TPU v7x, 256 devices: a whole 4x4x8 slice. The times are simulated.
256 devices in a mesh: grp: 32 (over y, z_lo, core), tp: 8 (over x, z_hi).
Axes of the slice: x: 4, y: 4, z: 8 (z_hi: 2, z_lo: 4; z = z_hi * 4 + z_lo), core: 2. Of those that a mesh axis runs over, the one named last changes fastest.
Arguments:
- tok_ids: int32 [8192], P('grp'), may hold values from 0 to 16383
- accept: int32 [8192], P('grp'), may hold values 0 or 1
- sub_ids: int32 [8192], P('grp'), may hold values from 0 to 16383
- cache_len: int32 [32], replicated, may hold values from 256 to 3840, as said below
- spill: int32 [32], replicated, may hold values from 0 to 1792, as said below
- embed: bfloat16 [16384, 2048], P('grp', 'tp'), may hold values from -6 to 6
- attn_gain: float32 [2048], replicated, may hold values from 0.25 to 1.75
- w_query: bfloat16 [2048, 2048], P(None, 'tp'), may hold values from -0.125 to 0.125
- w_key: bfloat16 [2048, 512], P(None, 'tp'), as said below
- w_value: bfloat16 [2048, 512], P(None, 'tp'), as said below
- w_out: bfloat16 [2048, 2048], P('tp'), may hold values from -2.5 to 2.5
- mlp_gain: float32 [2048], replicated, may hold values from 0.25 to 1.75
- w_gate: bfloat16 [2048, 5632], P(None, 'tp'), may hold values from -0.125 to 0.125
- w_up: bfloat16 [2048, 5632], P(None, 'tp'), may hold values from -0.125 to 0.125
- w_down: bfloat16 [5632, 2048], P('tp'), may hold values from -0.078125 to 0.078125
- cache_keys: bfloat16 [65536, 512], P('grp', 'tp'), may hold values from -320 to 320, as said below
- cache_values: bfloat16 [65536, 512], P('grp', 'tp'), may hold values from -8 to 8, as said below
Outputs:
- first_out: bfloat16 [8192, 2048], P('grp', 'tp')
- second_out: bfloat16 [8192, 2048], P('grp', 'tp')
Inputs may be any that keep to these rules, and one draw needn't show every extreme that they name: Request g keeps cache_len[g] - spill[g] >= 256 positions in slots from 0 of store g and spill[g] positions in the last slots of store (g xor 1); for every g, cache_len[g] - spill[g] + spill[g xor 1] <= 2048. Of each pair of groups 2k, 2k + 1 at most one has spill above 0. `w_key`: the 2 stored copies of a key-value head are equal. `w_value`: the 2 stored copies of a key-value head are equal. `cache_keys`: the 2 stored copies of a key-value head are equal. `cache_values`: the 2 stored copies of a key-value head are equal.
All inputs are finite; a program needn't handle non-finite values. No bound on the sum of `accept` on one device may be relied on, other than what follows from the above.
Results may differ from a plain program's by a relative error of at most 0.024.
Values may be sent and summed in bfloat16 or wider, within the bound.
No kernel may reach another device: no remote copies, remote signals or barrier semaphores. Data moves between devices by JAX's collectives and lax.ppermute only.
A program may use at most 128 MiB of HBM per device.

v0:
```python
import jax
import jax.numpy as jnp
from jax import lax
from jax.sharding import PartitionSpec as P

HD = 64
EPSILON = 1e-05
SENTINEL = -1e30


def swapped(array, axis, bit):
    return lax.ppermute(array, axis, [(i, i ^ 1 << bit) for i in range(lax.axis_size(axis))])


def rms_normed(values, gain):
    square = jnp.mean(values * values, axis=-1, keepdims=True)
    return (values * lax.rsqrt(square + EPSILON) * gain).astype(jnp.bfloat16)


def rotate(vectors, positions):
    half = vectors.shape[-1] // 2
    exponent = jnp.arange(half, dtype=jnp.float32) * (-2.0 / vectors.shape[-1])
    freqs = jnp.power(jnp.float32(10000.0), exponent)
    angles = positions.astype(jnp.float32)[:, None] * freqs[None, :]
    cosine = jnp.cos(angles)[:, None, :]
    sine = jnp.sin(angles)[:, None, :]
    first = vectors[..., :half]
    second = vectors[..., half:]
    return jnp.concatenate(
        [first * cosine - second * sine, second * cosine + first * sine], axis=-1
    )


def partial_attention(query, keys, values, valid):
    scores = jnp.einsum("bcgd,kcd->bcgk", query, keys, preferred_element_type=jnp.float32) * 0.125
    scores = jnp.where(valid, scores, SENTINEL)
    top = jnp.max(scores, axis=-1)
    weights = jnp.where(valid, jnp.exp(scores - top[..., None]), 0.0)
    total = jnp.sum(weights, axis=-1)
    weighted = jnp.einsum(
        "bcgk,kcd->bcgd", weights.astype(jnp.bfloat16), values, preferred_element_type=jnp.float32
    )
    return (weighted, top, total)


def on_device(
    tok_ids,
    accept,
    sub_ids,
    cache_len,
    spill,
    embed,
    attn_gain,
    w_query,
    w_key,
    w_value,
    w_out,
    mlp_gain,
    w_gate,
    w_up,
    w_down,
    cache_keys,
    cache_values,
):
    block = tok_ids.shape[0]
    slots = cache_keys.shape[0]
    local_vocab = embed.shape[0]
    query_local = w_query.shape[1] // HD
    stored_local = w_key.shape[1] // HD
    per_stored = query_local // stored_local
    group_index = lax.axis_index("grp")
    shard_index = lax.axis_index("tp")
    own_count = cache_len[group_index] - spill[group_index]
    far_count = spill[group_index]
    positions = cache_len[group_index] + jnp.arange(block, dtype=jnp.int32)
    slot_ids = jnp.arange(slots, dtype=jnp.int32)
    tail_ids = slot_ids[block:]
    store_keys = cache_keys.reshape(slots, stored_local, HD)
    store_values = cache_values.reshape(slots, stored_local, HD)
    block_valid = jnp.ones((block,), dtype=bool)
    second_ids = jnp.where(accept == 1, sub_ids, tok_ids)
    vocab_base = group_index * local_vocab
    vocab_ids = jnp.arange(local_vocab, dtype=jnp.int32)

    def lookup(id_list):
        onehot = (id_list[:, None] - vocab_base == vocab_ids[None, :]).astype(jnp.bfloat16)
        return jnp.dot(onehot, embed, preferred_element_type=jnp.float32)

    all_first, all_second = (
        lax.all_gather(tok_ids, "grp", axis=0, tiled=True),
        lax.all_gather(second_ids, "grp", axis=0, tiled=True),
    )
    first_rows = lax.psum_scatter(
        lookup(all_first).astype(jnp.bfloat16), "grp", scatter_dimension=0, tiled=True
    )
    second_rows = lax.psum_scatter(
        lookup(all_second).astype(jnp.bfloat16), "grp", scatter_dimension=0, tiled=True
    )
    tail_keys, tail_values = swapped((cache_keys[block:], cache_values[block:]), "grp", 0)
    far_keys = tail_keys.reshape(slots - block, stored_local, HD)
    far_values = tail_values.reshape(slots - block, stored_local, HD)
    far_valid = tail_ids >= slots - far_count

    def denoise(x_part):
        width = x_part.shape[1]
        x_full = lax.all_gather(x_part, "tp", axis=1, tiled=True)
        normed = rms_normed(x_full.astype(jnp.float32), attn_gain)
        query = rotate(
            jnp.dot(normed, w_query, preferred_element_type=jnp.float32).reshape(
                block, query_local, HD
            ),
            positions,
        )
        query = query.astype(jnp.bfloat16).reshape(block, stored_local, per_stored, HD)
        new_keys = rotate(
            jnp.dot(normed, w_key, preferred_element_type=jnp.float32).reshape(
                block, stored_local, HD
            ),
            positions,
        ).astype(jnp.bfloat16)
        new_values = (
            jnp.dot(normed, w_value, preferred_element_type=jnp.float32)
            .reshape(block, stored_local, HD)
            .astype(jnp.bfloat16)
        )
        own_valid = slot_ids < own_count
        keys = jnp.concatenate([store_keys, far_keys, new_keys], axis=0)
        values = jnp.concatenate([store_values, far_values, new_values], axis=0)
        valid = jnp.concatenate([own_valid, far_valid, block_valid])
        weighted, top, total = partial_attention(query, keys, values, valid)
        attended = weighted / total[..., None]
        mixed = attended.reshape(block, query_local * HD).astype(jnp.bfloat16)
        head_term = jnp.dot(mixed, w_out, preferred_element_type=jnp.float32)
        head_sum = lax.psum(head_term.astype(jnp.bfloat16), "tp").astype(jnp.float32)
        resid_full = (x_full.astype(jnp.float32) + head_sum).astype(jnp.bfloat16)
        resid_part = lax.dynamic_slice_in_dim(resid_full, shard_index * width, width, 1)
        normed_mlp = rms_normed(resid_full.astype(jnp.float32), mlp_gain)
        gate = jnp.dot(normed_mlp, w_gate, preferred_element_type=jnp.float32)
        lift = jnp.dot(normed_mlp, w_up, preferred_element_type=jnp.float32)
        hidden = (jax.nn.silu(gate) * lift).astype(jnp.bfloat16)
        down_term = jnp.dot(hidden, w_down, preferred_element_type=jnp.float32)
        down_part = lax.psum_scatter(
            down_term.astype(jnp.bfloat16), "tp", scatter_dimension=1, tiled=True
        ).astype(jnp.float32)
        return (resid_part.astype(jnp.float32) + down_part).astype(jnp.bfloat16)

    return (denoise(first_rows), denoise(second_rows))


def solution(mesh):
    placed = (
        P("grp"),
        P("grp"),
        P("grp"),
        P(),
        P(),
        P("grp", "tp"),
        P(),
        P(None, "tp"),
        P(None, "tp"),
        P(None, "tp"),
        P("tp", None),
        P(),
        P(None, "tp"),
        P(None, "tp"),
        P("tp", None),
        P("grp", "tp"),
        P("grp", "tp"),
    )
    return jax.shard_map(
        on_device,
        mesh=mesh,
        in_specs=placed,
        out_specs=(P("grp", "tp"), P("grp", "tp")),
        check_vma=False,
    )
```

profile of v0, /device:TPU:8, one launch (start us, length us, event | category | flops | bytes accessed | tf_op | source)
XLA Modules:
  0.0 960.8 jit_solution(10995285730689573226)
XLA Ops:
  8.1 37.6 %all-gather.1 = s32[32,1,256]{2,1,0:T(1,128)S(1)} all-gather(s32[1,1,256]{2,1,0:T(1,128)S(1)} %bitcast.193), channel_id=1, replica_groups=mesh['grp'=32,'tp'=8] {'grp'}, dimensions={0}, use_global_device_ids=true | all-gather | bytes 33792 | tf_op jit(solution)/shard_map/all_gather | solution.py:91
  45.7 38.2 %all-gather = s32[32,1,256]{2,1,0:T(1,128)S(1)} all-gather(s32[1,1,256]{2,1,0:T(1,128)} %bitcast.192), channel_id=1, replica_groups=mesh['grp'=32,'tp'=8] {'grp'}, dimensions={0}, use_global_device_ids=true | all-gather | bytes 33792 | tf_op jit(solution)/shard_map/all_gather | solution.py:90
  83.9 6.3 fusion.10
  91.1 5.4 fusion.11
  96.6 131.9 %reduce-scatter.9.cloned.1.call-done = bf16[256,256]{1,0:T(8,128)(2,1)} async-done(((bf16[8192,256]{1,0:T(8,128)(2,1)}), bf16[256,256]{1,0:T(8,128)(2,1)}) %reduce-scatter.9.cloned.1.call-update) | async-done | bytes 131088 | tf_op jit(solution)/shard_map/reduce_scatter | solution.py:96
  228.6 151.1 %reduce-scatter.5.cloned.1.call-done = bf16[256,256]{1,0:T(8,128)(2,1)} async-done(((bf16[8192,256]{1,0:T(8,128)(2,1)}), bf16[256,256]{1,0:T(8,128)(2,1)}) %reduce-scatter.5.cloned.1.call-update) | async-done | bytes 131088 | tf_op jit(solution)/shard_map/reduce_scatter | solution.py:93
  386.7 73.9 %all-gather.7.cloned.1.call-done = bf16[256,2048]{1,0:T(8,128)(2,1)} async-done(((bf16[256,256]{1,0:T(8,128)(2,1)}), bf16[256,2048]{1,0:T(8,128)(2,1)}) %all-gather.7.cloned.1.call-update) | async-done | bytes 1048592 | tf_op jit(solution)/shard_map/all_gather | solution.py:106
  462.1 58.2 %all-gather.5.cloned.1.call-done = bf16[256,2048]{1,0:T(8,128)(2,1)} async-done(((bf16[256,256]{1,0:T(8,128)(2,1)}), bf16[256,2048]{1,0:T(8,128)(2,1)}) %all-gather.5.cloned.1.call-update) | async-done | bytes 1048592 | tf_op jit(solution)/shard_map/all_gather | solution.py:106
  520.3 1.7 fusion.30
  522.0 2.3 fusion.114
  526.3 8.1 fusion.61
  534.5 14.5 %bitcast_reduce_fusion = (f32[256,4]{0,1:T(4,128)S(1)}, f32[256,4]{0,1:T(4,128)S(1)}, f32[4096,256,4]{1,0,2:T(8,128)}) fusion(pred[4096]{0:T(1024)(128)(4,1)S(1)} %pad_add_fusion, f32[4096,256,4]{1,0,2:T(8,128)} %fusion.61, bf16[256,4,32]{0,2,1:T(8,128)(2,1)S(1)} %get-tuple-element.13, bf16[256,4,32]{0,2,1:T(8,128)(2,1)S(1)} %get-tuple-element.12, ...), kind=kOutput, calls=%fused_computation.1 | convolution fusion | flops 564393984 | bytes 34222080 | tf_op jit(solution)/shard_map/bcgd,kcd->bcgk/dot_general | solution.py:35
  549.0 14.2 %fusion.8 = (f32[256,4]{0,1:T(4,128)S(1)}, f32[256,4]{0,1:T(4,128)S(1)}) fusion(f32[4096,256,4]{1,0,2:T(8,128)} %get-tuple-element.26, f32[256,4]{0,1:T(4,128)S(1)} %get-tuple-element.4, pred[4096]{0:T(1024)(128)(4,1)S(1)} %pad_add_fusion, f32[256,4]{0,1:T(4,128)S(1)} %get-tuple-element.5, f32[4096,256,4]{1,0,2:T(8,128)} %fusion.61), kind=kLoop, calls=%fused_computation.16 | loop fusion | flops 41940992 | bytes 33574912 | tf_op jit(solution)/shard_map/reduce_sum | solution.py:39
  563.8 5.4 fusion.51
  571.3 5.1 fusion.57
  578.2 190.4 %all-reduce.3.cloned.1.call-done = (bf16[256,2048]{1,0:T(8,128)(2,1)}, bf16[256,2048]{1,0:T(8,128)(2,1)}) async-done(((bf16[256,2048]{1,0:T(8,128)(2,1)}, bf16[256,2048]{1,0:T(8,128)(2,1)}), (bf16[256,2048]{1,0:T(8,128)(2,1)}, bf16[256,2048]{1,0:T(8,128)(2,1)})) %all-reduce.3.cloned.1.call-update) | async-done | bytes 2097168 | tf_op jit(solution)/shard_map/psum | solution.py:134
  768.6 2.2 fusion.24
  771.8 1.9 fusion.78
  773.8 6.6 convolution_convert_fusion.2
  780.5 2.2 fusion.27
  783.7 1.9 fusion.74
  785.6 6.6 convolution_convert_fusion
  792.3 72.7 %reduce-scatter.7.cloned.1.call-done = bf16[256,256]{1,0:T(8,128)(2,1)} async-done(((bf16[256,2048]{1,0:T(8,128)(2,1)}), bf16[256,256]{1,0:T(8,128)(2,1)}) %reduce-scatter.7.cloned.1.call-update) | async-done | bytes 131088 | tf_op jit(solution)/shard_map/reduce_scatter | solution.py:142
  866.6 85.6 %reduce-scatter.11.cloned.1.call-done = bf16[256,256]{1,0:T(8,128)(2,1)} async-done(((bf16[256,2048]{1,0:T(8,128)(2,1)}), bf16[256,256]{1,0:T(8,128)(2,1)}) %reduce-scatter.11.cloned.1.call-update) | async-done | bytes 131088 | tf_op jit(solution)/shard_map/reduce_scatter | solution.py:142
  (101 shorter events, 20.1 us)
Async XLA Ops:
  7.2 766.6 %copy-start = (bf16[704,2048]{1,0:T(8,128)(2,1)S(1)}, bf16[704,2048]{1,0:T(8,128)(2,1)}, u32[]{:S(2)}) copy-start(bf16[704,2048]{1,0:T(8,128)(2,1)} %param.31) | copy-start | bytes 8650756
  7.2 221.3 %reduce-scatter.9.cloned.1.call-start = ((), (), s32[]{:S(2)}) async-start(), calls=%async_computation.7 | async-start | bytes 4325376 | tf_op jit(solution)/shard_map/reduce_scatter | solution.py:96
  90.2 289.5 %reduce-scatter.5.cloned.1.call-start = ((), (), s32[]{:S(2)}) async-start(), calls=%async_computation.4 | async-start | bytes 4325376 | tf_op jit(solution)/shard_map/reduce_scatter | solution.py:93
  96.5 283.2 %copy-start.6 = (bf16[2048,64]{0,1:T(8,128)(2,1)S(1)}, bf16[2048,64]{0,1:T(8,128)(2,1)}, u32[]{:S(2)}) copy-start(bf16[2048,64]{0,1:T(8,128)(2,1)} %param.32) | copy-start | bytes 786436
  96.5 286.1 %copy-start.16 = (s32[32]{0:T(128)S(1)}, s32[32]{0:T(128)}, u32[]{:S(2)}) copy-start(s32[32]{0:T(128)} %param.20) | copy-start | bytes 388
  96.5 286.7 %copy-start.17 = (s32[32]{0:T(128)S(1)}, s32[32]{0:T(128)}, u32[]{:S(2)}) copy-start(s32[32]{0:T(128)} %param.21) | copy-start | bytes 388
  96.5 425.4 %copy-start.14 = (f32[2048]{0:T(1024)S(1)}, f32[2048]{0:T(1024)}, u32[]{:S(2)}) copy-start(f32[2048]{0:T(1024)} %param.23) | copy-start | bytes 24580
  96.6 364.0 %all-gather.7.cloned.1.call-start = ((), (), s32[]{:S(2)}) async-start(), calls=%async_computation.8 | async-start | bytes 1179648 | tf_op jit(solution)/shard_map/all_gather | solution.py:106
  228.5 291.7 %all-gather.5.cloned.1.call-start = ((), (), s32[]{:S(2)}) async-start(), calls=%async_computation.5 | async-start | bytes 1179648 | tf_op jit(solution)/shard_map/all_gather | solution.py:106
  379.7 388.9 %all-reduce.3.cloned.1.call-start = ((), (), s32[]{:S(2)}) async-start(), calls=%async_computation.10 | async-start | bytes 4194304 | tf_op jit(solution)/shard_map/psum | solution.py:134
  380.5 145.9 %collective-permute-start.1 = (bf16[1792,64]{0,1:T(8,128)(2,1)}, bf16[1792,64]{0,1:T(8,128)(2,1)S(1)}, u32[]{:S(2)}, u32[]{:S(2)}) collective-permute-start(bf16[1792,64]{0,1:T(8,128)(2,1)} %slice.35), channel_id=1, source_target_pairs={{0,8},{8,0},{16,24},{24,16},{32,40},{40,32},{48,56},{56,48},{64,72... | collective-permute-start | bytes 688136 | tf_op jit(solution)/shard_map/ppermute | solution.py:12
  382.1 181.6 %collective-permute-start = (bf16[1792,64]{0,1:T(8,128)(2,1)}, bf16[1792,64]{0,1:T(8,128)(2,1)}, u32[]{:S(2)}, u32[]{:S(2)}) collective-permute-start(bf16[1792,64]{0,1:T(8,128)(2,1)} %slice.33), channel_id=1, source_target_pairs={{0,8},{8,0},{16,24},{24,16},{32,40},{40,32},{48,56},{56,48},{64,72... | collective-permute-start | bytes 688136 | tf_op jit(solution)/shard_map/ppermute | solution.py:12
  534.5 29.3 %slice-start = ((s8[16777216]{0:T(1024)(128)(4,1)}), s8[4194304]{0:T(1024)(128)(4,1)S(1)}, s32[]{:S(2)}) async-start(s8[16777216]{0:T(1024)(128)(4,1)} %bitcast.174), calls=%async_computation.11 | async-start | bytes 8388608
  534.5 29.3 %slice-start.1 = ((s8[16777216]{0:T(1024)(128)(4,1)}), s8[4194304]{0:T(1024)(128)(4,1)S(1)}, s32[]{:S(2)}) async-start(s8[16777216]{0:T(1024)(128)(4,1)} %bitcast.174), calls=%async_computation.12 | async-start | bytes 8388608
  534.5 29.3 %slice-start.2 = ((s8[16777216]{0:T(1024)(128)(4,1)}), s8[4194304]{0:T(1024)(128)(4,1)S(1)}, s32[]{:S(2)}) async-start(s8[16777216]{0:T(1024)(128)(4,1)} %bitcast.174), calls=%async_computation.13 | async-start | bytes 8388608
  549.0 14.2 %copy-start.13 = (bf16[2048,64]{0,1:T(8,128)(2,1)S(1)}, bf16[2048,64]{0,1:T(8,128)(2,1)}, u32[]{:S(2)}) copy-start(bf16[2048,64]{0,1:T(8,128)(2,1)} %param.26) | copy-start | bytes 786436
  549.0 14.8 %slice-start.3 = ((s8[16777216]{0:T(1024)(128)(4,1)}), s8[4194304]{0:T(1024)(128)(4,1)S(1)}, s32[]{:S(2)}) async-start(s8[16777216]{0:T(1024)(128)(4,1)} %bitcast.174), calls=%async_computation.14 | async-start | bytes 8388608
  549.0 14.8 %copy-start.7 = (bf16[2048,64]{0,1:T(8,128)(2,1)S(1)}, bf16[2048,64]{0,1:T(8,128)(2,1)}, u32[]{:S(2)}) copy-start(bf16[2048,64]{0,1:T(8,128)(2,1)} %param.33) | copy-start | bytes 786436
  563.2 8.1 slice-start.4
  563.8 7.5 slice-start.5
  563.8 7.5 slice-start.6
  577.9 194.0 %copy-start.15 = (f32[2048]{0:T(1024)S(1)}, f32[2048]{0:T(1024)}, u32[]{:S(2)}) copy-start(f32[2048]{0:T(1024)} %param.28) | copy-start | bytes 24580
  577.9 287.1 %reduce-scatter.7.cloned.1.call-start = ((), (), s32[]{:S(2)}) async-start(), calls=%async_computation.6 | async-start | bytes 1179648 | tf_op jit(solution)/shard_map/reduce_scatter | solution.py:142
  780.5 171.8 %reduce-scatter.11.cloned.1.call-start = ((), (), s32[]{:S(2)}) async-start(), calls=%async_computation.9 | async-start | bytes 1179648 | tf_op jit(solution)/shard_map/reduce_scatter | solution.py:142
  (11 other events, 36.6 us)
Sparse Core Ops, SparseCore 0:
  90.3 138.1 reduce-scatter.8
  231.0 148.6 reduce-scatter.4
  382.2 78.3 all-gather.6
  462.9 57.3 all-gather.4
  578.0 190.5 all-reduce.2
  780.6 84.3 reduce-scatter.6
  869.4 82.7 reduce-scatter.10
where the time goes:
time: 961 us
  waiting for transfers between devices  764 us (80%)
  blocking collectives  75.8 us (8%)
  matrix products  70 us (7%)
  other arithmetic  27.1 us (3%)
  between operations  16.5 us (2%)
    psum x1, waiting for transfers between devices, denoise(): lax.psum(head_term.astype(jnp.bfloat16), 'tp').astype(jnp.float32)  190 us
    reduce_scatter x2, waiting for transfers between devices, denoise(): lax.psum_scatter(down_term.astype(jnp.bfloat16), 'tp', scatter_dimension=...  158 us
    reduce_scatter x1, waiting for transfers between devices, on_device(): lax.psum_scatter(lookup(all_first).astype(jnp.bfloat16), 'grp', scatter_d...  151 us
    all_gather x2, waiting for transfers between devices, denoise(): x_full = lax.all_gather(x_part, 'tp', axis=1, tiled=True)  132 us
    reduce_scatter x1, waiting for transfers between devices, on_device(): lax.psum_scatter(lookup(all_second).astype(jnp.bfloat16), 'grp', scatter_...  132 us
    all_gather x1, blocking collectives, on_device(): lax.all_gather(tok_ids, 'grp', axis=0, tiled=True)  38.2 us
    all_gather x1, blocking collectives, on_device(): lax.all_gather(second_ids, 'grp', axis=0, tiled=True)  37.6 us
    dot_general x2, matrix products, partial_attention(): jnp.einsum('bcgd,kcd->bcgk', query, keys, preferred_element_type=jnp.floa...  22.6 us
  transfers between devices with their start and end apart: 9, of which 7 were waited for; matrix products, arithmetic and copies ran while one was open for 7% of the time, Pallas kernels for 0%

commit v1 on v0

--- a/solution.py
+++ b/solution.py
@@ -6,6 +6,12 @@
 HD = 64
 EPSILON = 1e-05
 SENTINEL = -1e30
+
+
+def summed_here(x, name):
+    shards = lax.all_gather(x, name, axis=0, tiled=False)
+    result = shards.sum(axis=0)
+    return result
 
 
 def swapped(array, axis, bit):
@@ -131,7 +137,7 @@
         attended = weighted / total[..., None]
         mixed = attended.reshape(block, query_local * HD).astype(jnp.bfloat16)
         head_term = jnp.dot(mixed, w_out, preferred_element_type=jnp.float32)
-        head_sum = lax.psum(head_term.astype(jnp.bfloat16), "tp").astype(jnp.float32)
+        head_sum = summed_here(head_term.astype(jnp.bfloat16), "tp").astype(jnp.float32)
         resid_full = (x_full.astype(jnp.float32) + head_sum).astype(jnp.bfloat16)
         resid_part = lax.dynamic_slice_in_dim(resid_full, shard_index * width, width, 1)
         normed_mlp = rms_normed(resid_full.astype(jnp.float32), mlp_gain)

time: 961 us -> 1090 us (1.13)
  waiting for transfers between devices: 764 us -> 876 us
  other arithmetic: 27.1 us -> 39.8 us
    all_gather x0 -> x2, waiting for transfers between devices: none -> 309 us  [summed_here(): shards = lax.all_gather(x, name, axis=0, tiled=False)]
    psum x1 -> x0, waiting for transfers between devices: 190 us -> none  [denoise(): lax.psum(head_term.astype(jnp.bfloat16), 'tp').astype(jnp.float32)]
    reduce_sum x0 -> x2, other arithmetic: none -> 12.9 us  [summed_here(): result = shards.sum(axis=0)]
  transfers between devices with their start and end apart: 9 -> 10, of which waited for: 7 -> 8; matrix products, arithmetic and copies ran while one was open for 7% -> 9% of each run, Pallas kernels for 0% -> 0%
where the time goes in v1:
time: 1090 us
  waiting for transfers between devices  876 us (80%)
  blocking collectives  75.8 us (7%)
  matrix products  75 us (7%)
  other arithmetic  39.8 us (4%)
  between operations  16.4 us (2%)
    all_gather x2, waiting for transfers between devices, summed_here(): shards = lax.all_gather(x, name, axis=0, tiled=False)  309 us
    reduce_scatter x2, waiting for transfers between devices, denoise(): lax.psum_scatter(down_term.astype(jnp.bfloat16), 'tp', scatter_dimension=...  153 us
    reduce_scatter x1, waiting for transfers between devices, on_device(): lax.psum_scatter(lookup(all_first).astype(jnp.bfloat16), 'grp', scatter_d...  152 us
    reduce_scatter x1, waiting for transfers between devices, on_device(): lax.psum_scatter(lookup(all_second).astype(jnp.bfloat16), 'grp', scatter_...  131 us
    all_gather x2, waiting for transfers between devices, denoise(): x_full = lax.all_gather(x_part, 'tp', axis=1, tiled=True)  131 us
    all_gather x1, blocking collectives, on_device(): lax.all_gather(tok_ids, 'grp', axis=0, tiled=True)  38.2 us
    all_gather x1, blocking collectives, on_device(): lax.all_gather(second_ids, 'grp', axis=0, tiled=True)  37.6 us
    dot_general x2, matrix products, partial_attention(): jnp.einsum('bcgd,kcd->bcgk', query, keys, preferred_element_type=jnp.floa...  22.8 us
  transfers between devices with their start and end apart: 10, of which 8 were waited for; matrix products, arithmetic and copies ran while one was open for 9% of the time, Pallas kernels for 0%

profile of v1, /device:TPU:8, one launch (start us, length us, event | category | flops | bytes accessed | tf_op | source)
XLA Modules:
  0.0 1090.7 jit_solution(7703473463430343621)
XLA Ops:
  8.1 37.6 %all-gather.3 = s32[32,1,256]{2,1,0:T(1,128)S(1)} all-gather(s32[1,1,256]{2,1,0:T(1,128)S(1)} %bitcast.195), channel_id=1, replica_groups=mesh['grp'=32,'tp'=8] {'grp'}, dimensions={0}, use_global_device_ids=true | all-gather | bytes 33792 | tf_op jit(solution)/shard_map/all_gather | solution.py:97
  45.7 38.2 %all-gather.2 = s32[32,1,256]{2,1,0:T(1,128)S(1)} all-gather(s32[1,1,256]{2,1,0:T(1,128)} %bitcast.194), channel_id=1, replica_groups=mesh['grp'=32,'tp'=8] {'grp'}, dimensions={0}, use_global_device_ids=true | all-gather | bytes 33792 | tf_op jit(solution)/shard_map/all_gather | solution.py:96
  83.9 6.3 fusion.10
  91.1 5.4 fusion.11
  96.6 131.5 %reduce-scatter.9.cloned.1.call-done = bf16[256,256]{1,0:T(8,128)(2,1)} async-done(((bf16[8192,256]{1,0:T(8,128)(2,1)}), bf16[256,256]{1,0:T(8,128)(2,1)}) %reduce-scatter.9.cloned.1.call-update) | async-done | bytes 131088 | tf_op jit(solution)/shard_map/reduce_scatter | solution.py:102
  228.2 151.9 %reduce-scatter.5.cloned.1.call-done = bf16[256,256]{1,0:T(8,128)(2,1)} async-done(((bf16[8192,256]{1,0:T(8,128)(2,1)}), bf16[256,256]{1,0:T(8,128)(2,1)}) %reduce-scatter.5.cloned.1.call-update) | async-done | bytes 131088 | tf_op jit(solution)/shard_map/reduce_scatter | solution.py:99
  387.1 72.8 %all-gather.11.cloned.1.call-done = bf16[256,2048]{1,0:T(8,128)(2,1)} async-done(((bf16[256,256]{1,0:T(8,128)(2,1)}), bf16[256,2048]{1,0:T(8,128)(2,1)}) %all-gather.11.cloned.1.call-update) | async-done | bytes 1048592 | tf_op jit(solution)/shard_map/all_gather | solution.py:112
  461.4 58.2 %all-gather.9.cloned.1.call-done = bf16[256,2048]{1,0:T(8,128)(2,1)} async-done(((bf16[256,256]{1,0:T(8,128)(2,1)}), bf16[256,2048]{1,0:T(8,128)(2,1)}) %all-gather.9.cloned.1.call-update) | async-done | bytes 1048592 | tf_op jit(solution)/shard_map/all_gather | solution.py:112
  521.3 2.3 fusion.114
  525.7 8.1 fusion.61
  533.8 14.7 %bitcast_reduce_fusion = (f32[256,4]{0,1:T(4,128)S(1)}, f32[256,4]{0,1:T(4,128)S(1)}, f32[4096,256,4]{1,0,2:T(8,128)}) fusion(pred[4096]{0:T(1024)(128)(4,1)S(1)} %pad_add_fusion, f32[4096,256,4]{1,0,2:T(8,128)} %fusion.61, bf16[256,4,32]{0,2,1:T(8,128)(2,1)S(1)} %get-tuple-element.11, bf16[256,4,32]{0,2,1:T(8,128)(2,1)S(1)} %get-tuple-element.10, ...), kind=kOutput, calls=%fused_computation.1 | convolution fusion | flops 564393984 | bytes 34222080 | tf_op jit(solution)/shard_map/bcgd,kcd->bcgk/dot_general | solution.py:41
  548.5 14.0 %fusion.8 = (f32[256,4]{0,1:T(4,128)S(1)}, f32[256,4]{0,1:T(4,128)S(1)}) fusion(f32[4096,256,4]{1,0,2:T(8,128)} %get-tuple-element.24, f32[256,4]{0,1:T(4,128)S(1)} %get-tuple-element.4, pred[4096]{0:T(1024)(128)(4,1)S(1)} %pad_add_fusion, f32[256,4]{0,1:T(4,128)S(1)} %get-tuple-element.5, f32[4096,256,4]{1,0,2:T(8,128)} %fusion.61), kind=kLoop, calls=%fused_computation.16 | loop fusion | flops 41940992 | bytes 33574912 | tf_op jit(solution)/shard_map/reduce_sum | solution.py:45
  563.1 5.2 fusion.51
  571.6 8.9 fusion.57
  582.2 156.9 %all-gather.13.cloned.1.call-done = bf16[2048,2048]{1,0:T(8,128)(2,1)} async-done(((bf16[256,2048]{1,0:T(8,128)(2,1)}), bf16[2048,2048]{1,0:T(8,128)(2,1)}) %all-gather.13.cloned.1.call-update) | async-done | bytes 8388624 | tf_op jit(solution)/shard_map/all_gather | solution.py:12
  739.2 6.5 reduce_sum.80
  745.6 2.2 fusion.24
  750.9 6.7 convolution_convert_fusion.2
  757.9 151.7 %all-gather.15.cloned.1.call-done = bf16[2048,2048]{1,0:T(8,128)(2,1)} async-done(((bf16[256,2048]{1,0:T(8,128)(2,1)}), bf16[2048,2048]{1,0:T(8,128)(2,1)}) %all-gather.15.cloned.1.call-update) | async-done | bytes 8388624 | tf_op jit(solution)/shard_map/all_gather | solution.py:12
  909.7 6.4 reduce_sum.84
  916.0 2.2 fusion.27
  921.2 6.6 convolution_convert_fusion
  927.9 67.1 %reduce-scatter.7.cloned.1.call-done = bf16[256,256]{1,0:T(8,128)(2,1)} async-done(((bf16[256,2048]{1,0:T(8,128)(2,1)}), bf16[256,256]{1,0:T(8,128)(2,1)}) %reduce-scatter.7.cloned.1.call-update) | async-done | bytes 131088 | tf_op jit(solution)/shard_map/reduce_scatter | solution.py:148
  996.6 85.6 %reduce-scatter.11.cloned.1.call-done = bf16[256,256]{1,0:T(8,128)(2,1)} async-done(((bf16[256,2048]{1,0:T(8,128)(2,1)}), bf16[256,256]{1,0:T(8,128)(2,1)}) %reduce-scatter.11.cloned.1.call-update) | async-done | bytes 131088 | tf_op jit(solution)/shard_map/reduce_scatter | solution.py:148
  (99 shorter events, 27.3 us)
Async XLA Ops:
  7.2 743.7 %copy-start = (bf16[704,2048]{1,0:T(8,128)(2,1)S(1)}, bf16[704,2048]{1,0:T(8,128)(2,1)}, u32[]{:S(2)}) copy-start(bf16[704,2048]{1,0:T(8,128)(2,1)} %param.31) | copy-start | bytes 8650756
  7.2 220.9 %reduce-scatter.9.cloned.1.call-start = ((), (), s32[]{:S(2)}) async-start(), calls=%async_computation.7 | async-start | bytes 4325376 | tf_op jit(solution)/shard_map/reduce_scatter | solution.py:102
  90.2 289.9 %reduce-scatter.5.cloned.1.call-start = ((), (), s32[]{:S(2)}) async-start(), calls=%async_computation.4 | async-start | bytes 4325376 | tf_op jit(solution)/shard_map/reduce_scatter | solution.py:99
  96.5 283.6 %copy-start.7 = (bf16[2048,64]{0,1:T(8,128)(2,1)S(1)}, bf16[2048,64]{0,1:T(8,128)(2,1)}, u32[]{:S(2)}) copy-start(bf16[2048,64]{0,1:T(8,128)(2,1)} %param.32) | copy-start | bytes 786436
  96.5 286.5 %copy-start.17 = (s32[32]{0:T(128)S(1)}, s32[32]{0:T(128)}, u32[]{:S(2)}) copy-start(s32[32]{0:T(128)} %param.20) | copy-start | bytes 388
  96.5 287.1 %copy-start.18 = (s32[32]{0:T(128)S(1)}, s32[32]{0:T(128)}, u32[]{:S(2)}) copy-start(s32[32]{0:T(128)} %param.21) | copy-start | bytes 388
  96.5 424.7 %copy-start.15 = (f32[2048]{0:T(1024)S(1)}, f32[2048]{0:T(1024)}, u32[]{:S(2)}) copy-start(f32[2048]{0:T(1024)} %param.23) | copy-start | bytes 24580
  96.6 363.3 %all-gather.11.cloned.1.call-start = ((), (), s32[]{:S(2)}) async-start(), calls=%async_computation.8 | async-start | bytes 1179648 | tf_op jit(solution)/shard_map/all_gather | solution.py:112
  228.1 291.5 %all-gather.9.cloned.1.call-start = ((), (), s32[]{:S(2)}) async-start(), calls=%async_computation.5 | async-start | bytes 1179648 | tf_op jit(solution)/shard_map/all_gather | solution.py:112
  380.1 359.1 %all-gather.13.cloned.1.call-start = ((), (), s32[]{:S(2)}) async-start(), calls=%async_computation.10 | async-start | bytes 9437184 | tf_op jit(solution)/shard_map/all_gather | solution.py:12
  380.8 144.8 %collective-permute-start.1 = (bf16[1792,64]{0,1:T(8,128)(2,1)}, bf16[1792,64]{0,1:T(8,128)(2,1)S(1)}, u32[]{:S(2)}, u32[]{:S(2)}) collective-permute-start(bf16[1792,64]{0,1:T(8,128)(2,1)} %slice.35), channel_id=1, source_target_pairs={{0,8},{8,0},{16,24},{24,16},{32,40},{40,32},{48,56},{56,48},{64,72... | collective-permute-start | bytes 688136 | tf_op jit(solution)/shard_map/ppermute | solution.py:18
  382.5 180.5 %collective-permute-start = (bf16[1792,64]{0,1:T(8,128)(2,1)}, bf16[1792,64]{0,1:T(8,128)(2,1)}, u32[]{:S(2)}, u32[]{:S(2)}) collective-permute-start(bf16[1792,64]{0,1:T(8,128)(2,1)} %slice.33), channel_id=1, source_target_pairs={{0,8},{8,0},{16,24},{24,16},{32,40},{40,32},{48,56},{56,48},{64,72... | collective-permute-start | bytes 688136 | tf_op jit(solution)/shard_map/ppermute | solution.py:18
  519.6 4.0 copy-start.11
  533.8 29.2 %slice-start = ((s8[16777216]{0:T(1024)(128)(4,1)}), s8[4194304]{0:T(1024)(128)(4,1)S(1)}, s32[]{:S(2)}) async-start(s8[16777216]{0:T(1024)(128)(4,1)} %bitcast.176), calls=%async_computation.12 | async-start | bytes 8388608
  533.8 29.2 %slice-start.1 = ((s8[16777216]{0:T(1024)(128)(4,1)}), s8[4194304]{0:T(1024)(128)(4,1)S(1)}, s32[]{:S(2)}) async-start(s8[16777216]{0:T(1024)(128)(4,1)} %bitcast.176), calls=%async_computation.13 | async-start | bytes 8388608
  533.8 29.2 %slice-start.2 = ((s8[16777216]{0:T(1024)(128)(4,1)}), s8[4194304]{0:T(1024)(128)(4,1)S(1)}, s32[]{:S(2)}) async-start(s8[16777216]{0:T(1024)(128)(4,1)} %bitcast.176), calls=%async_computation.14 | async-start | bytes 8388608
  548.5 14.0 %copy-start.14 = (bf16[2048,64]{0,1:T(8,128)(2,1)S(1)}, bf16[2048,64]{0,1:T(8,128)(2,1)}, u32[]{:S(2)}) copy-start(bf16[2048,64]{0,1:T(8,128)(2,1)} %param.26) | copy-start | bytes 786436
  548.5 14.5 %slice-start.3 = ((s8[16777216]{0:T(1024)(128)(4,1)}), s8[4194304]{0:T(1024)(128)(4,1)S(1)}, s32[]{:S(2)}) async-start(s8[16777216]{0:T(1024)(128)(4,1)} %bitcast.176), calls=%async_computation.15 | async-start | bytes 8388608
  548.5 14.5 %copy-start.8 = (bf16[2048,64]{0,1:T(8,128)(2,1)S(1)}, bf16[2048,64]{0,1:T(8,128)(2,1)}, u32[]{:S(2)}) copy-start(bf16[2048,64]{0,1:T(8,128)(2,1)} %param.33) | copy-start | bytes 786436
  563.0 5.2 copy-start.1
  569.8 339.8 %all-gather.15.cloned.1.call-start = ((), (), s32[]{:S(2)}) async-start(), calls=%async_computation.11 | async-start | bytes 9437184 | tf_op jit(solution)/shard_map/all_gather | solution.py:12
  571.6 8.9 copy-start.2
  581.9 413.0 %reduce-scatter.7.cloned.1.call-start = ((), (), s32[]{:S(2)}) async-start(), calls=%async_computation.6 | async-start | bytes 1179648 | tf_op jit(solution)/shard_map/reduce_scatter | solution.py:148
  757.6 324.6 %reduce-scatter.11.cloned.1.call-start = ((), (), s32[]{:S(2)}) async-start(), calls=%async_computation.9 | async-start | bytes 1179648 | tf_op jit(solution)/shard_map/reduce_scatter | solution.py:148
  (9 other events, 23.0 us)
Sparse Core Ops, SparseCore 0:
  90.3 137.7 reduce-scatter.8
  230.6 149.4 reduce-scatter.4
  382.6 77.2 all-gather.10
  462.2 57.3 all-gather.8
  569.9 169.1 all-gather.12
  741.6 167.9 all-gather.14
  913.6 81.3 reduce-scatter.6
  999.4 82.7 reduce-scatter.10
